TPU v7x, 32 devices: a whole 2x2x4 slice. The times are simulated.
32 devices in a mesh: groups: 2 (over y), bricks: 4 (over z), heads: 4 (over x, core).
Axes of the slice: x: 2, y: 2, z: 4, core: 2. Of those that a mesh axis runs over, the one named last changes fastest.
Arguments:
- voxel_feats: bfloat16 [4096, 1024], P(('groups', 'bricks'), 'heads'), parts along dimension 0, may hold values from -6 to 6
- face_open: int32 [8], P('groups'), parts along dimension 0, may hold values from 0 to 1
- pattern: int32 [8, 4], P('groups'), parts along dimension 0, may hold values from 0 to 1, as said below
- conv_weight: bfloat16 [27, 1024], P(None, 'heads'), may hold values from -1.25 to 1.25
- conv_bias: bfloat16 [1024], P('heads'), may hold values from -0.5 to 0.5
- gain_one: bfloat16 [1024], replicated, may hold values from 0.099609375 to 1.8984375
- query_weight: bfloat16 [1024, 1024], P(None, 'heads'), may hold values from -3 to 3
- key_weight: bfloat16 [1024, 1024], P(None, 'heads'), may hold values from -3 to 3
- value_weight: bfloat16 [1024, 1024], P(None, 'heads'), may hold values from -0.1875 to 0.1875
- out_weight: bfloat16 [1024, 1024], P('heads'), may hold values from -0.1875 to 0.1875
- gain_two: bfloat16 [1024], replicated, may hold values from 0.099609375 to 1.8984375
- up_weight: bfloat16 [1024, 4096], P(None, 'heads'), may hold values from -0.1875 to 0.1875
- down_weight: bfloat16 [4096, 1024], P('heads'), may hold values from -0.09375 to 0.09375
Outputs:
- block_out: bfloat16 [4096, 1024], P(('groups', 'bricks'), 'heads'), parts along dimension 0
There are 2 independent parts, one for each index of `groups`. A program takes and returns all parts, laid end to end along the dimension named above; an argument that names none is the same for every part. Nothing has to cross between parts.
Inputs may be any that keep to these rules, and one draw needn't show every extreme that they name: pattern is 0 or 1; every brick attends to itself; each query brick attends to 3 or more key bricks, and some query brick to all 4.
All inputs are finite; a program needn't handle non-finite values.
Results may differ from a plain program's by a relative error of at most 0.012.
Values may be sent and summed in bfloat16 or wider, within the bound.
No kernel may reach another device: no remote copies, remote signals or barrier semaphores. Data moves between devices by JAX's collectives and lax.ppermute only.
A program may use at most 64 MiB of HBM per device.

v0:
```python
import jax
import jax.numpy as jnp
from jax import lax
from jax.sharding import PartitionSpec as P

EDGE = 8
HEAD_DIM = 64
epsilon = 1e-05


def extended_2(value, sides, width):
    for axis, dim in sides:
        size, length = (lax.axis_size(axis), value.shape[dim])
        up = [(i, (i + 1) % size) for i in range(size - 1)]
        down = [(j, i) for i, j in up]
        last = lax.slice_in_dim(value, length - width, length, axis=dim)
        first = lax.slice_in_dim(value, 0, width, axis=dim)
        before = lax.ppermute(last, axis, up)
        after = lax.ppermute(first, axis, down)
        value = jnp.concatenate([before, value, after], axis=dim)
    return value


def layer_norm(inputs, gain_vec):
    values = inputs.astype(jnp.float32)
    center = values - jnp.mean(values, axis=-1, keepdims=True)
    spread = jnp.mean(center * center, axis=-1, keepdims=True)
    return center * lax.rsqrt(spread + epsilon) * gain_vec.astype(jnp.float32)


def depthwise(brick_vals, lower_face, upper_face, conv_weight, conv_bias):
    brick_count = brick_vals.shape[0]
    edge_len = brick_vals.shape[1]
    channels = brick_vals.shape[3]
    layers = jnp.concatenate([lower_face[:, None], brick_vals, upper_face[:, None]], axis=1)
    layers = layers.reshape(brick_count, edge_len + 2, edge_len, edge_len, channels)
    padded = jnp.pad(layers, ((0, 0), (0, 0), (1, 1), (1, 1), (0, 0)))
    weights = conv_weight.astype(jnp.float32)
    summed = jnp.zeros((brick_count, edge_len, edge_len, edge_len, channels), jnp.float32)
    for step_x in range(3):
        for step_y in range(3):
            for step_z in range(3):
                window = padded[
                    :,
                    step_x : step_x + edge_len,
                    step_y : step_y + edge_len,
                    step_z : step_z + edge_len,
                ]
                summed = summed + weights[step_x * 9 + step_y * 3 + step_z] * window
    return summed.reshape(brick_count * edge_len**3, channels) + conv_bias.astype(jnp.float32)


def shards(
    voxel_feats,
    face_open,
    pattern,
    conv_weight,
    conv_bias,
    gain_one,
    query_weight,
    key_weight,
    value_weight,
    out_weight,
    gain_two,
    up_weight,
    down_weight,
):
    row_count = voxel_feats.shape[0]
    local_width = voxel_feats.shape[1]
    face_rows = EDGE * EDGE
    brick_rows = EDGE * face_rows
    local_bricks = row_count // brick_rows
    brick_total = pattern.shape[0]
    first_brick = lax.axis_index("bricks") * local_bricks
    extended = extended_2(voxel_feats, (("bricks", 0),), face_rows)
    brick_vals = extended[face_rows : face_rows + row_count].astype(jnp.float32)
    brick_vals = brick_vals.reshape(local_bricks, EDGE, face_rows, local_width)
    lower_face = jnp.concatenate(
        [extended[:face_rows].astype(jnp.float32)[None], brick_vals[:-1, EDGE - 1]], axis=0
    )
    upper_face = jnp.concatenate(
        [brick_vals[1:, 0], extended[face_rows + row_count :].astype(jnp.float32)[None]], axis=0
    )
    brick_ids = first_brick + jnp.arange(local_bricks, dtype=jnp.int32)
    lower_open = jnp.where(brick_ids >= 1, jnp.take(face_open, brick_ids), 0)
    upper_open = jnp.where(
        brick_ids + 1 < brick_total,
        jnp.take(face_open, jnp.minimum(brick_ids + 1, brick_total - 1)),
        0,
    )
    lower_face = lower_face * lower_open.astype(jnp.float32)[:, None, None]
    upper_face = upper_face * upper_open.astype(jnp.float32)[:, None, None]
    conv_out = depthwise(brick_vals, lower_face, upper_face, conv_weight, conv_bias)
    stream = (voxel_feats.astype(jnp.float32) + conv_out).astype(jnp.bfloat16)
    stream_full = lax.all_gather(stream, "heads", axis=1, tiled=True)
    normed = layer_norm(stream_full, gain_one).astype(jnp.bfloat16)
    queries = jnp.dot(normed, query_weight, preferred_element_type=jnp.float32).astype(jnp.bfloat16)
    head_count = local_width // HEAD_DIM
    query_heads = queries.reshape(local_bricks, brick_rows, head_count, HEAD_DIM)
    score_scale = HEAD_DIM ** (-0.5)
    start_state = (
        jnp.full((local_bricks, head_count, brick_rows), -1e30, jnp.float32),
        jnp.zeros((local_bricks, head_count, brick_rows), jnp.float32),
        jnp.zeros((local_bricks, brick_rows, head_count, HEAD_DIM), jnp.float32),
    )

    def absorb(state_in, local_id, key_brick, fetch_pair):
        linked = pattern[first_brick + local_id, key_brick]

        def include(state_now):
            row_max, row_mass, weighted = state_now
            key_rows, value_rows = fetch_pair()
            keys_h = key_rows.reshape(brick_rows, head_count, HEAD_DIM)
            values_h = value_rows.reshape(brick_rows, head_count, HEAD_DIM)
            query_one = lax.dynamic_index_in_dim(query_heads, local_id, 0, keepdims=False)
            scores = (
                jnp.einsum("qhd,khd->hqk", query_one, keys_h, preferred_element_type=jnp.float32)
                * score_scale
            )
            max_old = lax.dynamic_index_in_dim(row_max, local_id, 0, keepdims=False)
            mass_old = lax.dynamic_index_in_dim(row_mass, local_id, 0, keepdims=False)
            sum_old = lax.dynamic_index_in_dim(weighted, local_id, 0, keepdims=False)
            max_new = jnp.maximum(max_old, jnp.max(scores, axis=-1))
            factor = jnp.exp(max_old - max_new)
            weights = jnp.exp(scores - max_new[:, :, None])
            mass_new = mass_old * factor + jnp.sum(weights, axis=-1)
            sum_new = sum_old * jnp.transpose(factor)[:, :, None] + jnp.einsum(
                "hqk,khd->qhd",
                weights.astype(jnp.bfloat16),
                values_h,
                preferred_element_type=jnp.float32,
            )
            return (
                lax.dynamic_update_index_in_dim(row_max, max_new, local_id, 0),
                lax.dynamic_update_index_in_dim(row_mass, mass_new, local_id, 0),
                lax.dynamic_update_index_in_dim(weighted, sum_new, local_id, 0),
            )

        return lax.cond(linked > 0, include, lambda state_now: state_now, state_in)

    keys_all = jnp.dot(normed, key_weight, preferred_element_type=jnp.float32).astype(jnp.bfloat16)
    values_all = jnp.dot(normed, value_weight, preferred_element_type=jnp.float32).astype(
        jnp.bfloat16
    )
    key_piece = lax.all_gather(keys_all, "bricks", axis=0, tiled=True)
    value_piece = lax.all_gather(values_all, "bricks", axis=0, tiled=True)
    piece_bricks = key_piece.shape[0] // brick_rows

    def visit(visit_idx, state_now):
        local_id = visit_idx // piece_bricks
        offset = visit_idx % piece_bricks

        def fetch_pair():
            return (
                lax.dynamic_slice_in_dim(key_piece, offset * brick_rows, brick_rows, 0),
                lax.dynamic_slice_in_dim(value_piece, offset * brick_rows, brick_rows, 0),
            )

        return absorb(state_now, local_id, offset, fetch_pair)

    result = lax.fori_loop(0, local_bricks * piece_bricks, visit, start_state)
    row_max, row_mass, weighted = result
    attended = (weighted / jnp.transpose(row_mass, (0, 2, 1))[:, :, :, None]).astype(jnp.bfloat16)
    attended = attended.reshape(row_count, local_width)
    partial_out = jnp.dot(attended, out_weight, preferred_element_type=jnp.float32)
    full_sum = lax.psum(partial_out.astype(jnp.bfloat16), "heads").astype(jnp.float32)
    stream_two_full = (stream_full.astype(jnp.float32) + full_sum).astype(jnp.bfloat16)
    stream_two = lax.dynamic_slice_in_dim(
        stream_two_full, lax.axis_index("heads") * local_width, local_width, 1
    )
    normed_two = layer_norm(stream_two_full, gain_two).astype(jnp.bfloat16)
    hidden = jax.nn.gelu(
        jnp.dot(normed_two, up_weight, preferred_element_type=jnp.float32), approximate=True
    ).astype(jnp.bfloat16)
    lowered = jnp.dot(hidden, down_weight, preferred_element_type=jnp.float32)
    mixed = lax.psum_scatter(
        lowered.astype(jnp.bfloat16), "heads", scatter_dimension=1, tiled=True
    ).astype(jnp.float32)
    return (stream_two.astype(jnp.float32) + mixed).astype(jnp.bfloat16)


def solution(mesh):
    return jax.shard_map(
        shards,
        mesh=mesh,
        in_specs=(
            P(("groups", "bricks"), "heads"),
            P("groups"),
            P("groups", None),
            P(None, "heads"),
            P("heads"),
            P(),
            P(None, "heads"),
            P(None, "heads"),
            P(None, "heads"),
            P("heads", None),
            P(),
            P(None, "heads"),
            P("heads", None),
        ),
        out_specs=P(("groups", "bricks"), "heads"),
        check_vma=False,
    )
```

profile of v0, /device:TPU:0, one launch (start us, length us, event | category | flops | bytes accessed | tf_op | source)
XLA Modules:
  0.0 208.5 jit_solution(12115050096938499187)
XLA Ops:
  6.5 0.9 fusion.95
  7.5 1.3 collective-permute-start.1
  8.8 5.6 %collective-permute-start = (bf16[64,256]{1,0:T(8,128)(2,1)S(1)}, bf16[64,256]{1,0:T(8,128)(2,1)S(1)}, u32[]{:S(2)}, u32[]{:S(2)}) collective-permute-start(bf16[64,256]{1,0:T(8,128)(2,1)S(1)} %get-tuple-element.350), channel_id=1, source_target_pairs={{0,4},{4,8},{8,12},{1,5},{5,9},{9,13},{2,6},{6,10},{10,14},{3,7},{... | collective-permute-start | bytes 98312 | tf_op jit(solution)/shard_map/ppermute | solution.py:18
  14.3 1.0 fusion.96
  15.3 0.9 fusion.97
  16.2 1.4 fusion.98
  18.3 1.0 convert.1
  20.9 1.6 fusion.57
  22.5 0.8 fusion.86
  23.4 17.6 %all-gather.4.cloned.1.call-done = bf16[512,1024]{1,0:T(8,128)(2,1)} async-done(((bf16[512,256]{1,0:T(8,128)(2,1)}), bf16[512,1024]{1,0:T(8,128)(2,1)}) %all-gather.4.cloned.1.call-update) | async-done | bytes 1048592 | tf_op jit(solution)/shard_map/all_gather | solution.py:95
  41.0 1.5 convert_reduce_fusion
  42.5 1.6 fusion.25
  44.2 2.3 %convolution_convert_fusion.4 = bf16[512,256]{1,0:T(8,128)(2,1)} fusion(bf16[1024,256]{1,0:T(8,128)(2,1)} %param.24, bf16[512,1024]{1,0:T(8,128)(2,1)S(1)} %copy-done.1, f32[1024]{0:T(1024)S(1)} %convert_element_type.108, f32[512]{0:T(512)S(1)} %add_rsqrt_fusion.1, f32[512]{0:T(512)S(1)} %broadcast_multiply_fusion.1), kind=kOutput, calls=%fused_computation.61 | convolution fusion | flops 271187968 | bytes 1843200 | tf_op jit(solution)/shard_map/dot_general | solution.py:141
  46.5 2.3 %convolution_convert_fusion.2 = bf16[512,256]{1,0:T(8,128)(2,1)} fusion(bf16[1024,256]{1,0:T(8,128)(2,1)} %param.25, bf16[512,1024]{1,0:T(8,128)(2,1)S(1)} %copy-done.1, f32[1024]{0:T(1024)S(1)} %convert_element_type.108, f32[512]{0:T(512)S(1)} %add_rsqrt_fusion.1, f32[512]{0:T(512)S(1)} %broadcast_multiply_fusion.1), kind=kOutput, calls=%fused_computation.59 | convolution fusion | flops 271187968 | bytes 1843200 | tf_op jit(solution)/shard_map/dot_general | solution.py:142
  48.8 1.7 convolution_convert_fusion.3
  50.6 24.0 %all-gather.6.cloned.1.call-done = bf16[2048,256]{1,0:T(8,128)(2,1)} async-done(((bf16[512,256]{1,0:T(8,128)(2,1)}), bf16[2048,256]{1,0:T(8,128)(2,1)}) %all-gather.6.cloned.1.call-update) | async-done | bytes 1048592 | tf_op jit(solution)/shard_map/all_gather | solution.py:145
  74.5 2.3 %copy.15 = bf16[2048,256]{0,1:T(8,128)(2,1)} copy(bf16[2048,256]{1,0:T(8,128)(2,1)} %all-gather.6.cloned.1.call-done) | data formatting | bytes 2097152 | tf_op jit(solution)/shard_map/while | solution.py:161
  76.8 26.8 %all-gather.8.cloned.1.call-done = bf16[2048,256]{1,0:T(8,128)(2,1)} async-done(((bf16[512,256]{1,0:T(8,128)(2,1)}), bf16[2048,256]{1,0:T(8,128)(2,1)}) %all-gather.8.cloned.1.call-update) | async-done | bytes 1048592 | tf_op jit(solution)/shard_map/all_gather | solution.py:146
  103.6 2.3 %copy.16 = bf16[2048,256]{0,1:T(8,128)(2,1)} copy(bf16[2048,256]{1,0:T(8,128)(2,1)} %all-gather.8.cloned.1.call-done) | data formatting | bytes 2097152 | tf_op jit(solution)/shard_map/while | solution.py:161
  105.9 22.0 %while.21 = (s32[]{:T(128)}, f32[1,4,512]{2,1,0:T(4,128)S(1)}, f32[1,4,512]{2,1,0:T(4,128)S(1)}, f32[1,512,4,64]{1,3,2,0:T(8,128)S(1)}, s32[]{:T(128)}, /*index=...) while((s32[]{:T(128)}, f32[1,4,512]{2,1,0:T(4,128)S(1)}, ...), condition=%wide.region_7.8_spmd, body=%wide.region_2.0_spmd.sunk | while | flops 277094432 | bytes 15589916 | solution.py:161
  106.0 1.3 dynamic_slice.33
  107.9 3.5 %conditional.2 = ((f32[1,4,512]{2,1,0:T(4,128)S(1)}, f32[1,4,512]{2,1,0:T(4,128)S(1)}, f32[1,512,4,64]{1,3,2,0:T(8,128)S(1)})) conditional(s32[]{:T(128)} %bitcast.111, (f32[1,4,512]{2,1,0:T(4,128)S(1)}, f32[1,4,512]{2,1,0:T(4,128)S(1)}, f32[1,512,4,64]{1,3,2,0:T(8,128)S(1)}) %tuple.92, (s32[]{:T(128)}, bf16[2048,256]{0,1:T(8,128)(2,1)}, ...), branch_computations={%region_3.3_spmd, %region_4.6_spmd} | conditional | flops 277094400 | bytes 15589458 | solution.py:139
  107.9 1.1 constant_dynamic-slice_fusion
  109.0 0.8 bitcast_reduce_fusion
  110.5 0.9 fusion.13
  111.5 1.3 dynamic_slice.33
  113.4 3.5 %conditional.2 = ((f32[1,4,512]{2,1,0:T(4,128)S(1)}, f32[1,4,512]{2,1,0:T(4,128)S(1)}, f32[1,512,4,64]{1,3,2,0:T(8,128)S(1)})) conditional(s32[]{:T(128)} %bitcast.111, (f32[1,4,512]{2,1,0:T(4,128)S(1)}, f32[1,4,512]{2,1,0:T(4,128)S(1)}, f32[1,512,4,64]{1,3,2,0:T(8,128)S(1)}) %tuple.92, (s32[]{:T(128)}, bf16[2048,256]{0,1:T(8,128)(2,1)}, ...), branch_computations={%region_3.3_spmd, %region_4.6_spmd} | conditional | flops 277094400 | bytes 15589458 | solution.py:139
  113.4 1.1 constant_dynamic-slice_fusion
  114.5 0.8 bitcast_reduce_fusion
  115.3 0.7 fusion.2
  116.0 0.9 fusion.13
  117.0 1.3 dynamic_slice.33
  118.9 3.5 %conditional.2 = ((f32[1,4,512]{2,1,0:T(4,128)S(1)}, f32[1,4,512]{2,1,0:T(4,128)S(1)}, f32[1,512,4,64]{1,3,2,0:T(8,128)S(1)})) conditional(s32[]{:T(128)} %bitcast.111, (f32[1,4,512]{2,1,0:T(4,128)S(1)}, f32[1,4,512]{2,1,0:T(4,128)S(1)}, f32[1,512,4,64]{1,3,2,0:T(8,128)S(1)}) %tuple.92, (s32[]{:T(128)}, bf16[2048,256]{0,1:T(8,128)(2,1)}, ...), branch_computations={%region_3.3_spmd, %region_4.6_spmd} | conditional | flops 277094400 | bytes 15589458 | solution.py:139
  118.9 1.1 constant_dynamic-slice_fusion
  120.0 0.8 bitcast_reduce_fusion
  121.5 0.9 fusion.13
  122.5 1.3 dynamic_slice.33
  124.4 3.5 %conditional.2 = ((f32[1,4,512]{2,1,0:T(4,128)S(1)}, f32[1,4,512]{2,1,0:T(4,128)S(1)}, f32[1,512,4,64]{1,3,2,0:T(8,128)S(1)})) conditional(s32[]{:T(128)} %bitcast.111, (f32[1,4,512]{2,1,0:T(4,128)S(1)}, f32[1,4,512]{2,1,0:T(4,128)S(1)}, f32[1,512,4,64]{1,3,2,0:T(8,128)S(1)}) %tuple.92, (s32[]{:T(128)}, bf16[2048,256]{0,1:T(8,128)(2,1)}, ...), branch_computations={%region_3.3_spmd, %region_4.6_spmd} | conditional | flops 277094400 | bytes 15589458 | solution.py:139
  124.4 1.1 constant_dynamic-slice_fusion
  125.5 0.8 bitcast_reduce_fusion
  127.0 0.9 fusion.13
  128.0 2.6 %convolution_convert_fusion.1 = bf16[512,1024]{1,0:T(8,128)(2,1)} fusion(bf16[512,256]{0,1:T(8,128)(2,1)S(1)} %bitcast.116, bf16[256,1024]{1,0:T(8,128)(2,1)} %param.26), kind=kOutput, calls=%fused_computation.58 | convolution fusion | flops 268959744 | bytes 1835008 | tf_op jit(solution)/shard_map/dot_general | solution.py:165
  130.7 35.7 %all-reduce.3.cloned.1.call-done = bf16[512,1024]{1,0:T(8,128)(2,1)} async-done(((bf16[512,1024]{1,0:T(8,128)(2,1)}), bf16[512,1024]{1,0:T(8,128)(2,1)}) %all-reduce.3.cloned.1.call-update) | async-done | bytes 1048592 | tf_op jit(solution)/shard_map/psum | solution.py:166
  166.4 1.6 convert_reduce_fusion.1
  168.0 1.0 copy-done.3
  169.4 5.4 %convolution_convert_fusion = bf16[512,1024]{1,0:T(8,128)(2,1)} fusion(bf16[1024,1024]{1,0:T(8,128)(2,1)S(1)} %copy-done, bf16[1024,1024]{1,0:T(8,128)(2,1)} %param.28, bf16[512,1024]{1,0:T(8,128)(2,1)} %copy-done.3, f32[1024]{0:T(1024)S(1)} %convert_element_type.119, f32[512]{0:T(512)S(1)} %add_rsqrt_fusion, f32[512]{0:T(512)S(1)} %broadcast_multiply_fusion), kind=kOutput, calls=%fused_computation.57 | convolution fusion | flops 2155347968 | bytes 6299648 | tf_op jit(solution)/shard_map/dot_general | solution.py:175
  174.8 25.4 %reduce-scatter.2.cloned.1.call-done = bf16[512,256]{1,0:T(8,128)(2,1)} async-done(((bf16[512,1024]{1,0:T(8,128)(2,1)}), bf16[512,256]{1,0:T(8,128)(2,1)}) %reduce-scatter.2.cloned.1.call-update) | async-done | bytes 262160 | tf_op jit(solution)/shard_map/reduce_scatter | solution.py:176
  200.2 1.8 add_convert_fusion
  (51 shorter events, 4.0 us)
Async XLA Ops:
  6.5 162.8 %copy-start = (bf16[1024,1024]{1,0:T(8,128)(2,1)S(1)}, bf16[1024,1024]{1,0:T(8,128)(2,1)}, u32[]{:S(2)}) copy-start(bf16[1024,1024]{1,0:T(8,128)(2,1)} %param.29) | copy-start | bytes 6291460
  6.5 34.4 %all-gather.4.cloned.1.call-start = ((), (), s32[]{:S(2)}) async-start(), calls=%async_computation.1 | async-start | bytes 1310720 | tf_op jit(solution)/shard_map/all_gather | solution.py:95
  7.5 13.1 %collective-permute-start.1 = (bf16[64,256]{1,0:T(8,128)(2,1)S(1)}, bf16[64,256]{1,0:T(8,128)(2,1)S(1)}, u32[]{:S(2)}, u32[]{:S(2)}) collective-permute-start(bf16[64,256]{1,0:T(8,128)(2,1)S(1)} %get-tuple-element.351), channel_id=1, source_target_pairs={{4,0},{8,4},{12,8},{5,1},{9,5},{13,9},{6,2},{10,6},{14,10},{7,3},{... | collective-permute-start | bytes 98312 | tf_op jit(solution)/shard_map/ppermute | solution.py:19
  8.8 11.8 %collective-permute-start = (bf16[64,256]{1,0:T(8,128)(2,1)S(1)}, bf16[64,256]{1,0:T(8,128)(2,1)S(1)}, u32[]{:S(2)}, u32[]{:S(2)}) collective-permute-start(bf16[64,256]{1,0:T(8,128)(2,1)S(1)} %get-tuple-element.350), channel_id=1, source_target_pairs={{0,4},{4,8},{8,12},{1,5},{5,9},{9,13},{2,6},{6,10},{10,14},{3,7},{... | collective-permute-start | bytes 98312 | tf_op jit(solution)/shard_map/ppermute | solution.py:18
  20.9 1.6 copy-start.4
  20.9 2.5 %copy-start.5 = (bf16[1024]{0:T(1024)(128)(2,1)S(1)}, bf16[1024]{0:T(1024)(128)(2,1)}, u32[]{:S(2)}) copy-start(bf16[1024]{0:T(1024)(128)(2,1)} %param.22) | copy-start | bytes 6148
  23.3 51.2 %all-gather.6.cloned.1.call-start = ((), (), s32[]{:S(2)}) async-start(), calls=%async_computation.2 | async-start | bytes 1310720 | tf_op jit(solution)/shard_map/all_gather | solution.py:145
  41.0 3.2 %copy-start.1 = (bf16[512,1024]{1,0:T(8,128)(2,1)S(1)}, bf16[512,1024]{1,0:T(8,128)(2,1)}, u32[]{:S(2)}) copy-start(bf16[512,1024]{1,0:T(8,128)(2,1)} %all-gather.4.cloned.1.call-done) | copy-start | bytes 3145732
  46.4 57.1 %all-gather.8.cloned.1.call-start = ((), (), s32[]{:S(2)}) async-start(), calls=%async_computation.3 | async-start | bytes 1310720 | tf_op jit(solution)/shard_map/all_gather | solution.py:146
  48.8 117.6 %all-reduce.3.cloned.1.call-start = ((), (), s32[]{:S(2)}) async-start(), calls=%async_computation.4 | async-start | bytes 2097152 | tf_op jit(solution)/shard_map/psum | solution.py:166
  127.9 2.7 %copy-start.6 = (bf16[1024]{0:T(1024)(128)(2,1)S(1)}, bf16[1024]{0:T(1024)(128)(2,1)}, u32[]{:S(2)}) copy-start(bf16[1024]{0:T(1024)(128)(2,1)} %param.27) | copy-start | bytes 6148
  128.0 38.3 %copy-start.2 = (bf16[512,1024]{1,0:T(8,128)(2,1)S(1)}, bf16[512,1024]{1,0:T(8,128)(2,1)}, u32[]{:S(2)}) copy-start(bf16[512,1024]{1,0:T(8,128)(2,1)} %all-gather.4.cloned.1.call-done) | copy-start | bytes 3145732
  130.6 69.5 %reduce-scatter.2.cloned.1.call-start = ((), (), s32[]{:S(2)}) async-start(), calls=%async_computation.5 | async-start | bytes 1310720 | tf_op jit(solution)/shard_map/reduce_scatter | solution.py:176
  168.0 1.0 copy-start.3
Sparse Core Ops, SparseCore 0:
  23.4 17.5 all-gather.3
  46.6 27.9 all-gather.5
  76.1 27.4 all-gather.7
  130.7 35.5 all-reduce.2
  174.9 25.2 reduce-scatter.1
where the time goes:
time: 209 us; the launch traced here: 208 us
  waiting for transfers between devices  129 us (62%)
  matrix products  21 us (10%)
  local copies, waits for them, and re-layouts  19.2 us (9%)
  between operations  14.6 us (7%)
  other arithmetic  14.3 us (7%)
  starting transfers between devices  7.01 us (3%)
  loops' own time  2.85 us (1%)
    psum x1, waiting for transfers between devices, shards(): lax.psum(partial_out.astype(jnp.bfloat16), 'heads').astype(jnp.float32)  35.7 us
    all_gather x1, waiting for transfers between devices, shards(): value_piece = lax.all_gather(values_all, 'bricks', axis=0, tiled=True)  26.8 us
    reduce_scatter x1, waiting for transfers between devices, shards(): lax.psum_scatter(lowered.astype(jnp.bfloat16), 'heads', scatter_dimension...  25.4 us
    all_gather x1, waiting for transfers between devices, shards(): key_piece = lax.all_gather(keys_all, 'bricks', axis=0, tiled=True)  24 us
    all_gather x1, waiting for transfers between devices, shards(): stream_full = lax.all_gather(stream, 'heads', axis=1, tiled=True)  17.6 us
    ppermute x1, starting transfers between devices, extended_2(): before = lax.ppermute(last, axis, up)  5.56 us
    dot_general x1, matrix products, shards(): lowered = jnp.dot(hidden, down_weight, preferred_element_type=jnp.float32)  5.37 us
    dynamic_slice x4, local copies, waits for them, and re-layouts, absorb(): linked = pattern[first_brick + local_id, key_brick]  5.15 us
  transfers between devices with their start and end apart: 7, of which 5 were waited for; matrix products, arithmetic and copies ran while one was open for 5% of the time, Pallas kernels for 0%

commit v1 on v0

--- a/solution.py
+++ b/solution.py
@@ -6,6 +6,14 @@
 EDGE = 8
 HEAD_DIM = 64
 epsilon = 1e-05
+
+
+def work_zones(piece_in, axis_k):
+    piece_in = jnp.moveaxis(piece_in, 0, axis_k)
+    fresh = piece_in.shape
+    return piece_in.reshape(
+        *fresh[:axis_k], fresh[axis_k] * fresh[axis_k + 1], *fresh[axis_k + 2 :]
+    )
 
 
 def extended_2(value, sides, width):
@@ -142,7 +150,23 @@
     values_all = jnp.dot(normed, value_weight, preferred_element_type=jnp.float32).astype(
         jnp.bfloat16
     )
-    key_piece = lax.all_gather(keys_all, "bricks", axis=0, tiled=True)
+    axis_total = lax.axis_size("bricks")
+    block_list = tuple(((pp, (pp + 1) % axis_total) for pp in range(axis_total)))
+    arrivals = tuple(((d, ix) for ix, d in block_list))
+    e_next, block_out = ([], [])
+    for to_i in [*range(axis_total - 1)]:
+        if to_i % 2 == 0:
+            w_next = lax.ppermute(e_next[-1] if e_next else keys_all, "bricks", block_list)
+            e_next.append(w_next)
+        else:
+            mat_out = lax.ppermute(block_out[-1] if block_out else keys_all, "bricks", arrivals)
+            block_out.append(mat_out)
+    tile_out = jnp.stack([*e_next[::-1], keys_all, *block_out], axis=0)
+    a_now = len(e_next)
+    high = lax.axis_index("bricks")
+    lower = high - a_now
+    tile_out = tile_out[(jnp.arange(axis_total) - lower) % axis_total]
+    key_piece = work_zones(tile_out, 0)
     value_piece = lax.all_gather(values_all, "bricks", axis=0, tiled=True)
     piece_bricks = key_piece.shape[0] // brick_rows
 

time: 209 us -> 197 us (0.943)
  waiting for transfers between devices: 129 us -> 108 us
  starting transfers between devices: 7.01 us -> 13.6 us
    all_gather x1, waiting for transfers between devices: 26.8 us -> 0.01 us  [shards(): value_piece = lax.all_gather(values_all, 'bricks', axis=0, tiled=True)]
    ppermute x0 -> x3, waiting for transfers between devices: none -> 25.8 us  [the longest x1 13.6 us: shards(): lax.ppermute(block_out[-1] if block_out else keys_all, 'bricks', arrivals)]
    all_gather x1 -> x0, waiting for transfers between devices: 24 us -> none  [shards(): key_piece = lax.all_gather(keys_all, 'bricks', axis=0, tiled=True)]
    ppermute x0 -> x3, starting transfers between devices: none -> 6.63 us  [the longest x2 4.23 us: shards(): lax.ppermute(e_next[-1] if e_next else keys_all, 'bricks', block_list)]
    psum x1, waiting for transfers between devices: 35.7 us -> 38.7 us  [shards(): lax.psum(partial_out.astype(jnp.bfloat16), 'heads').astype(jnp.float32)]
  transfers between devices with their start and end apart: 7 -> 9, of which waited for: 5 -> 6; matrix products, arithmetic and copies ran while one was open for 5% -> 7% of each run, Pallas kernels for 0% -> 0%
where the time goes in v1:
time: 197 us; the launch traced here: 196 us
  waiting for transfers between devices  108 us (55%)
  matrix products  21 us (11%)
  local copies, waits for them, and re-layouts  20.8 us (11%)
  other arithmetic  15.5 us (8%)
  between operations  14.6 us (7%)
  starting transfers between devices  13.6 us (7%)
  loops' own time  2.85 us (1%)
    psum x1, waiting for transfers between devices, shards(): lax.psum(partial_out.astype(jnp.bfloat16), 'heads').astype(jnp.float32)  38.7 us
    reduce_scatter x1, waiting for transfers between devices, shards(): lax.psum_scatter(lowered.astype(jnp.bfloat16), 'heads', scatter_dimension...  25.4 us
    all_gather x1, waiting for transfers between devices, shards(): stream_full = lax.all_gather(stream, 'heads', axis=1, tiled=True)  17.6 us
    ppermute x1, waiting for transfers between devices, shards(): lax.ppermute(block_out[-1] if block_out else keys_all, 'bricks', arrivals)  13.6 us
    ppermute x2, waiting for transfers between devices, shards(): lax.ppermute(e_next[-1] if e_next else keys_all, 'bricks', block_list)  12.2 us
    ppermute x1, starting transfers between devices, extended_2(): before = lax.ppermute(last, axis, up)  5.56 us
    dot_general x1, matrix products, shards(): lowered = jnp.dot(hidden, down_weight, preferred_element_type=jnp.float32)  5.36 us
    dynamic_slice x4, local copies, waits for them, and re-layouts, absorb(): linked = pattern[first_brick + local_id, key_brick]  5.15 us
  transfers between devices with their start and end apart: 9, of which 6 were waited for; matrix products, arithmetic and copies ran while one was open for 7% of the time, Pallas kernels for 0%

profile of v1, /device:TPU:0, one launch (start us, length us, event | category | flops | bytes accessed | tf_op | source)
XLA Modules:
  0.0 196.0 jit_solution(14588108056731772593)
XLA Ops:
  6.5 0.9 fusion.97
  7.5 1.3 collective-permute-start.1
  8.8 5.6 %collective-permute-start = (bf16[64,256]{1,0:T(8,128)(2,1)S(1)}, bf16[64,256]{1,0:T(8,128)(2,1)S(1)}, u32[]{:S(2)}, u32[]{:S(2)}) collective-permute-start(bf16[64,256]{1,0:T(8,128)(2,1)S(1)} %get-tuple-element.350), channel_id=1, source_target_pairs={{0,4},{4,8},{8,12},{1,5},{5,9},{9,13},{2,6},{6,10},{10,14},{3,7},{... | collective-permute-start | bytes 98312 | tf_op jit(solution)/shard_map/ppermute | solution.py:26
  14.3 1.0 fusion.98
  15.3 0.9 fusion.99
  16.2 1.4 fusion.100
  18.3 1.0 convert.2
  20.9 1.6 fusion.57
  23.4 17.6 %all-gather.3.cloned.1.call-done = bf16[512,1024]{1,0:T(8,128)(2,1)} async-done(((bf16[512,256]{1,0:T(8,128)(2,1)}), bf16[512,1024]{1,0:T(8,128)(2,1)}) %all-gather.3.cloned.1.call-update) | async-done | bytes 1048592 | tf_op jit(solution)/shard_map/all_gather | solution.py:103
  41.0 1.5 convert_reduce_fusion
  42.5 1.6 fusion.25
  44.2 2.3 %convolution_convert_fusion.2 = bf16[512,256]{1,0:T(8,128)(2,1)} fusion(bf16[1024,256]{1,0:T(8,128)(2,1)} %param.25, bf16[512,1024]{1,0:T(8,128)(2,1)S(1)} %copy-done.1, f32[1024]{0:T(1024)S(1)} %convert_element_type.108, f32[512]{0:T(512)S(1)} %add_rsqrt_fusion.1, f32[512]{0:T(512)S(1)} %broadcast_multiply_fusion.1), kind=kOutput, calls=%fused_computation.60 | convolution fusion | flops 271187968 | bytes 1843200 | tf_op jit(solution)/shard_map/dot_general | solution.py:150
  46.5 2.3 %convolution_convert_fusion.4 = bf16[512,256]{1,0:T(8,128)(2,1)} fusion(bf16[1024,256]{1,0:T(8,128)(2,1)} %param.24, bf16[512,1024]{1,0:T(8,128)(2,1)S(1)} %copy-done.1, f32[1024]{0:T(1024)S(1)} %convert_element_type.108, f32[512]{0:T(512)S(1)} %add_rsqrt_fusion.1, f32[512]{0:T(512)S(1)} %broadcast_multiply_fusion.1), kind=kOutput, calls=%fused_computation.62 | convolution fusion | flops 271187968 | bytes 1843200 | tf_op jit(solution)/shard_map/dot_general | solution.py:149
  48.8 1.5 collective-permute-start.2
  50.3 2.4 %collective-permute-start.4 = (bf16[512,256]{1,0:T(8,128)(2,1)}, bf16[512,256]{1,0:T(8,128)(2,1)S(1)}, u32[]{:S(2)}, u32[]{:S(2)}) collective-permute-start(bf16[512,256]{1,0:T(8,128)(2,1)} %convolution_convert_fusion.4), channel_id=1, source_target_pairs={{4,0},{8,4},{12,8},{0,12},{5,1},{9,5},{13,9},{1,13},{6,2},{10,6},{... | collective-permute-start | bytes 786440 | tf_op jit(solution)/shard_map/ppermute | solution.py:162
  52.7 8.6 %collective-permute-done.2 = bf16[512,256]{1,0:T(8,128)(2,1)} collective-permute-done((bf16[512,256]{1,0:T(8,128)(2,1)}, bf16[512,256]{1,0:T(8,128)(2,1)}, u32[]{:S(2)}, u32[]{:S(2)}) %collective-permute-start.2) | collective-permute-done | bytes 262176 | tf_op jit(solution)/shard_map/ppermute | solution.py:159
  61.2 2.7 %collective-permute-start.3 = (bf16[512,256]{1,0:T(8,128)(2,1)}, bf16[512,256]{1,0:T(8,128)(2,1)S(1)}, u32[]{:S(2)}, u32[]{:S(2)}) collective-permute-start(bf16[512,256]{1,0:T(8,128)(2,1)} %collective-permute-done.2), channel_id=1, source_target_pairs={{0,4},{4,8},{8,12},{12,0},{1,5},{5,9},{9,13},{13,1},{2,6},{6,10},{... | collective-permute-start | bytes 786440 | tf_op jit(solution)/shard_map/ppermute | solution.py:159
  64.0 1.7 convolution_convert_fusion.3
  65.7 13.6 %collective-permute-done.4 = bf16[512,256]{1,0:T(8,128)(2,1)S(1)} collective-permute-done((bf16[512,256]{1,0:T(8,128)(2,1)}, bf16[512,256]{1,0:T(8,128)(2,1)S(1)}, u32[]{:S(2)}, u32[]{:S(2)}) %collective-permute-start.4) | collective-permute-done | bytes 262176 | tf_op jit(solution)/shard_map/ppermute | solution.py:162
  79.3 3.7 %collective-permute-done.3 = bf16[512,256]{1,0:T(8,128)(2,1)S(1)} collective-permute-done((bf16[512,256]{1,0:T(8,128)(2,1)}, bf16[512,256]{1,0:T(8,128)(2,1)S(1)}, u32[]{:S(2)}, u32[]{:S(2)}) %collective-permute-start.3) | collective-permute-done | bytes 262176 | tf_op jit(solution)/shard_map/ppermute | solution.py:159
  83.0 1.2 pad_maximum_fusion
  84.1 1.6 gather_fusion
  85.7 2.3 %copy.15 = bf16[2048,256]{0,1:T(8,128)(2,1)} copy(bf16[2048,256]{1,0:T(8,128)(2,1)} %bitcast.122) | data formatting | bytes 2097152 | tf_op jit(solution)/shard_map/while | solution.py:185
  88.0 2.3 %copy.16 = bf16[2048,256]{0,1:T(8,128)(2,1)} copy(bf16[2048,256]{1,0:T(8,128)(2,1)} %all-gather.5.cloned.1.call-done) | data formatting | bytes 2097152 | tf_op jit(solution)/shard_map/while | solution.py:185
  90.3 22.0 %while.21 = (s32[]{:T(128)}, f32[1,4,512]{2,1,0:T(4,128)S(1)}, f32[1,4,512]{2,1,0:T(4,128)S(1)}, f32[1,512,4,64]{1,3,2,0:T(8,128)S(1)}, s32[]{:T(128)}, /*index=...) while((s32[]{:T(128)}, f32[1,4,512]{2,1,0:T(4,128)S(1)}, ...), condition=%wide.region_7.8_spmd, body=%wide.region_2.0_spmd.sunk | while | flops 277094432 | bytes 15589916 | solution.py:185
  90.4 1.3 dynamic_slice.33
  92.3 3.5 %conditional.2 = ((f32[1,4,512]{2,1,0:T(4,128)S(1)}, f32[1,4,512]{2,1,0:T(4,128)S(1)}, f32[1,512,4,64]{1,3,2,0:T(8,128)S(1)})) conditional(s32[]{:T(128)} %bitcast.118, (f32[1,4,512]{2,1,0:T(4,128)S(1)}, f32[1,4,512]{2,1,0:T(4,128)S(1)}, f32[1,512,4,64]{1,3,2,0:T(8,128)S(1)}) %tuple.92, (s32[]{:T(128)}, bf16[2048,256]{0,1:T(8,128)(2,1)}, ...), branch_computations={%region_3.3_spmd, %region_4.6_spmd} | conditional | flops 277094400 | bytes 15589458 | solution.py:147
  92.3 1.1 constant_dynamic-slice_fusion
  94.9 0.9 fusion.13
  95.9 1.3 dynamic_slice.33
  97.8 3.5 %conditional.2 = ((f32[1,4,512]{2,1,0:T(4,128)S(1)}, f32[1,4,512]{2,1,0:T(4,128)S(1)}, f32[1,512,4,64]{1,3,2,0:T(8,128)S(1)})) conditional(s32[]{:T(128)} %bitcast.118, (f32[1,4,512]{2,1,0:T(4,128)S(1)}, f32[1,4,512]{2,1,0:T(4,128)S(1)}, f32[1,512,4,64]{1,3,2,0:T(8,128)S(1)}) %tuple.92, (s32[]{:T(128)}, bf16[2048,256]{0,1:T(8,128)(2,1)}, ...), branch_computations={%region_3.3_spmd, %region_4.6_spmd} | conditional | flops 277094400 | bytes 15589458 | solution.py:147
  97.8 1.1 constant_dynamic-slice_fusion
  100.4 0.9 fusion.13
  101.4 1.3 dynamic_slice.33
  103.3 3.5 %conditional.2 = ((f32[1,4,512]{2,1,0:T(4,128)S(1)}, f32[1,4,512]{2,1,0:T(4,128)S(1)}, f32[1,512,4,64]{1,3,2,0:T(8,128)S(1)})) conditional(s32[]{:T(128)} %bitcast.118, (f32[1,4,512]{2,1,0:T(4,128)S(1)}, f32[1,4,512]{2,1,0:T(4,128)S(1)}, f32[1,512,4,64]{1,3,2,0:T(8,128)S(1)}) %tuple.92, (s32[]{:T(128)}, bf16[2048,256]{0,1:T(8,128)(2,1)}, ...), branch_computations={%region_3.3_spmd, %region_4.6_spmd} | conditional | flops 277094400 | bytes 15589458 | solution.py:147
  103.3 1.1 constant_dynamic-slice_fusion
  105.9 0.9 fusion.13
  106.9 1.3 dynamic_slice.33
  108.8 3.5 %conditional.2 = ((f32[1,4,512]{2,1,0:T(4,128)S(1)}, f32[1,4,512]{2,1,0:T(4,128)S(1)}, f32[1,512,4,64]{1,3,2,0:T(8,128)S(1)})) conditional(s32[]{:T(128)} %bitcast.118, (f32[1,4,512]{2,1,0:T(4,128)S(1)}, f32[1,4,512]{2,1,0:T(4,128)S(1)}, f32[1,512,4,64]{1,3,2,0:T(8,128)S(1)}) %tuple.92, (s32[]{:T(128)}, bf16[2048,256]{0,1:T(8,128)(2,1)}, ...), branch_computations={%region_3.3_spmd, %region_4.6_spmd} | conditional | flops 277094400 | bytes 15589458 | solution.py:147
  108.8 1.1 constant_dynamic-slice_fusion
  111.4 0.9 fusion.13
  112.4 2.6 %convolution_convert_fusion.1 = bf16[512,1024]{1,0:T(8,128)(2,1)} fusion(bf16[512,256]{0,1:T(8,128)(2,1)S(1)} %bitcast.124, bf16[256,1024]{1,0:T(8,128)(2,1)} %param.26), kind=kOutput, calls=%fused_computation.59 | convolution fusion | flops 268959744 | bytes 1835008 | tf_op jit(solution)/shard_map/dot_general | solution.py:189
  115.1 38.7 %all-reduce.3.cloned.1.call-done = bf16[512,1024]{1,0:T(8,128)(2,1)} async-done(((bf16[512,1024]{1,0:T(8,128)(2,1)}), bf16[512,1024]{1,0:T(8,128)(2,1)}) %all-reduce.3.cloned.1.call-update) | async-done | bytes 1048592 | tf_op jit(solution)/shard_map/psum | solution.py:190
  153.8 1.6 convert_reduce_fusion.1
  155.4 1.0 copy-done.3
  156.8 5.4 %convolution_convert_fusion = bf16[512,1024]{1,0:T(8,128)(2,1)} fusion(bf16[1024,1024]{1,0:T(8,128)(2,1)S(1)} %copy-done, bf16[1024,1024]{1,0:T(8,128)(2,1)} %param.28, bf16[512,1024]{1,0:T(8,128)(2,1)} %copy-done.3, f32[1024]{0:T(1024)S(1)} %convert_element_type.119, f32[512]{0:T(512)S(1)} %add_rsqrt_fusion, f32[512]{0:T(512)S(1)} %broadcast_multiply_fusion), kind=kOutput, calls=%fused_computation.58 | convolution fusion | flops 2155347968 | bytes 6299648 | tf_op jit(solution)/shard_map/dot_general | solution.py:199
  162.2 25.4 %reduce-scatter.2.cloned.1.call-done = bf16[512,256]{1,0:T(8,128)(2,1)} async-done(((bf16[512,1024]{1,0:T(8,128)(2,1)}), bf16[512,256]{1,0:T(8,128)(2,1)}) %reduce-scatter.2.cloned.1.call-update) | async-done | bytes 262160 | tf_op jit(solution)/shard_map/reduce_scatter | solution.py:200
  187.7 1.8 add_convert_fusion
  (58 shorter events, 8.5 us)
Async XLA Ops:
  6.5 150.3 %copy-start = (bf16[1024,1024]{1,0:T(8,128)(2,1)S(1)}, bf16[1024,1024]{1,0:T(8,128)(2,1)}, u32[]{:S(2)}) copy-start(bf16[1024,1024]{1,0:T(8,128)(2,1)} %param.29) | copy-start | bytes 6291460
  6.5 34.4 %all-gather.3.cloned.1.call-start = ((), (), s32[]{:S(2)}) async-start(), calls=%async_computation.1 | async-start | bytes 1310720 | tf_op jit(solution)/shard_map/all_gather | solution.py:103
  7.5 13.1 %collective-permute-start.1 = (bf16[64,256]{1,0:T(8,128)(2,1)S(1)}, bf16[64,256]{1,0:T(8,128)(2,1)S(1)}, u32[]{:S(2)}, u32[]{:S(2)}) collective-permute-start(bf16[64,256]{1,0:T(8,128)(2,1)S(1)} %get-tuple-element.351), channel_id=1, source_target_pairs={{4,0},{8,4},{12,8},{5,1},{9,5},{13,9},{6,2},{10,6},{14,10},{7,3},{... | collective-permute-start | bytes 98312 | tf_op jit(solution)/shard_map/ppermute | solution.py:27
  8.8 11.8 %collective-permute-start = (bf16[64,256]{1,0:T(8,128)(2,1)S(1)}, bf16[64,256]{1,0:T(8,128)(2,1)S(1)}, u32[]{:S(2)}, u32[]{:S(2)}) collective-permute-start(bf16[64,256]{1,0:T(8,128)(2,1)S(1)} %get-tuple-element.350), channel_id=1, source_target_pairs={{0,4},{4,8},{8,12},{1,5},{5,9},{9,13},{2,6},{6,10},{10,14},{3,7},{... | collective-permute-start | bytes 98312 | tf_op jit(solution)/shard_map/ppermute | solution.py:26
  20.9 1.6 copy-start.4
  20.9 2.5 %copy-start.5 = (bf16[1024]{0:T(1024)(128)(2,1)S(1)}, bf16[1024]{0:T(1024)(128)(2,1)}, u32[]{:S(2)}) copy-start(bf16[1024]{0:T(1024)(128)(2,1)} %param.22) | copy-start | bytes 6148
  23.3 64.7 %all-gather.5.cloned.1.call-start = ((), (), s32[]{:S(2)}) async-start(), calls=%async_computation.2 | async-start | bytes 1310720 | tf_op jit(solution)/shard_map/all_gather | solution.py:170
  41.0 3.2 %copy-start.1 = (bf16[512,1024]{1,0:T(8,128)(2,1)S(1)}, bf16[512,1024]{1,0:T(8,128)(2,1)}, u32[]{:S(2)}) copy-start(bf16[512,1024]{1,0:T(8,128)(2,1)} %all-gather.3.cloned.1.call-done) | copy-start | bytes 3145732
  46.4 107.4 %all-reduce.3.cloned.1.call-start = ((), (), s32[]{:S(2)}) async-start(), calls=%async_computation.3 | async-start | bytes 2097152 | tf_op jit(solution)/shard_map/psum | solution.py:190
  48.8 12.5 %collective-permute-start.2 = (bf16[512,256]{1,0:T(8,128)(2,1)}, bf16[512,256]{1,0:T(8,128)(2,1)}, u32[]{:S(2)}, u32[]{:S(2)}) collective-permute-start(bf16[512,256]{1,0:T(8,128)(2,1)} %convolution_convert_fusion.4), channel_id=1, source_target_pairs={{0,4},{4,8},{8,12},{12,0},{1,5},{5,9},{9,13},{13,1},{2,6},{6,10},{... | collective-permute-start | bytes 786440 | tf_op jit(solution)/shard_map/ppermute | solution.py:159
  50.3 29.0 %collective-permute-start.4 = (bf16[512,256]{1,0:T(8,128)(2,1)}, bf16[512,256]{1,0:T(8,128)(2,1)S(1)}, u32[]{:S(2)}, u32[]{:S(2)}) collective-permute-start(bf16[512,256]{1,0:T(8,128)(2,1)} %convolution_convert_fusion.4), channel_id=1, source_target_pairs={{4,0},{8,4},{12,8},{0,12},{5,1},{9,5},{13,9},{1,13},{6,2},{10,6},{... | collective-permute-start | bytes 786440 | tf_op jit(solution)/shard_map/ppermute | solution.py:162
  61.2 21.7 %collective-permute-start.3 = (bf16[512,256]{1,0:T(8,128)(2,1)}, bf16[512,256]{1,0:T(8,128)(2,1)S(1)}, u32[]{:S(2)}, u32[]{:S(2)}) collective-permute-start(bf16[512,256]{1,0:T(8,128)(2,1)} %collective-permute-done.2), channel_id=1, source_target_pairs={{0,4},{4,8},{8,12},{12,0},{1,5},{5,9},{9,13},{13,1},{2,6},{6,10},{... | collective-permute-start | bytes 786440 | tf_op jit(solution)/shard_map/ppermute | solution.py:159
  112.3 2.7 %copy-start.6 = (bf16[1024]{0:T(1024)(128)(2,1)S(1)}, bf16[1024]{0:T(1024)(128)(2,1)}, u32[]{:S(2)}) copy-start(bf16[1024]{0:T(1024)(128)(2,1)} %param.27) | copy-start | bytes 6148
  112.4 41.4 %copy-start.2 = (bf16[512,1024]{1,0:T(8,128)(2,1)S(1)}, bf16[512,1024]{1,0:T(8,128)(2,1)}, u32[]{:S(2)}) copy-start(bf16[512,1024]{1,0:T(8,128)(2,1)} %all-gather.3.cloned.1.call-done) | copy-start | bytes 3145732
  115.0 72.7 %reduce-scatter.2.cloned.1.call-start = ((), (), s32[]{:S(2)}) async-start(), calls=%async_computation.4 | async-start | bytes 1310720 | tf_op jit(solution)/shard_map/reduce_scatter | solution.py:200
  155.4 1.0 copy-start.3
Sparse Core Ops, SparseCore 0:
  23.4 17.5 all-gather.2
  46.6 41.0 all-gather.4
  115.1 38.6 all-reduce.2
  162.3 25.2 reduce-scatter.1
